TPU v7x, 256 devices: a whole 4x4x8 slice. The times are simulated.
256 devices in a mesh: row: 8 (over y_hi, x), col: 32 (over y_lo, z, core).
Axes of the slice: x: 4, y: 4 (y_hi: 2, y_lo: 2; y = y_hi * 2 + y_lo), z: 8, core: 2. Of those that a mesh axis runs over, the one named last changes fastest.
Arguments:
- left_image: bfloat16 [64, 16384, 128], P('row', 'col'), may hold values from -9 to 9
- right_image: bfloat16 [64, 16384, 128], P('row', 'col'), may hold values from -9 to 9
- conv_weight: bfloat16 [3, 3, 128, 256], replicated, may hold values from -0.1875 to 0.1875
Outputs:
- disparity: float32 [32, 8192], P('row', 'col')
- entropy: float32 [32, 8192], P('row', 'col')
All inputs are finite; a program needn't handle non-finite values.
Results may differ from a plain program's by a relative error of at most 0.0057.
Values may be sent and summed in bfloat16 or wider, within the bound.
No kernel may reach another device: no remote copies, remote signals or barrier semaphores. Data moves between devices by JAX's collectives and lax.ppermute only.
A program may use at most 64 MiB of HBM per device.

v0:
```python
import jax
import jax.numpy as jnp
from jax import lax
from jax.sharding import PartitionSpec as P

NEG_FILL = -1e30


def from_behind(array, axis, by):
    count = lax.axis_size(axis)
    pairs = [(i, i + by) for i in range(count) if 0 <= i + by < count]
    return lax.ppermute(array, axis, pairs)


def conv_taps(padded, weights, row_count, col_count):
    total = jnp.zeros((row_count * col_count, weights.shape[-1]), jnp.float32)
    for a in range(3):
        for b in range(3):
            window = padded[a : a + 2 * row_count - 1 : 2, b : b + 2 * col_count - 1 : 2, :]
            total = total + jnp.dot(
                window.reshape(row_count * col_count, -1),
                weights[a, b],
                preferred_element_type=jnp.float32,
            )
    return total.astype(jnp.bfloat16).reshape(row_count, col_count, -1)


def empty_state(row_count, col_count):
    zeros = jnp.zeros((row_count, col_count), jnp.float32)
    return (jnp.full((row_count, col_count), NEG_FILL, jnp.float32), zeros, zeros, zeros)


def absorb(state, query, panel_keys, offset):
    peak, mass, moment, spread = state
    scores = jnp.einsum(
        "rif,rjf->rij", query, panel_keys, preferred_element_type=jnp.float32
    ) * query.shape[-1] ** (-0.5)
    offset = jnp.asarray(offset, jnp.int32).astype(jnp.float32)
    distance = (
        offset
        + jnp.arange(query.shape[1], dtype=jnp.float32)[:, None]
        - jnp.arange(panel_keys.shape[1], dtype=jnp.float32)[None, :]
    )
    allowed = distance >= 0.0
    block_peak = jnp.max(jnp.where(allowed, scores, NEG_FILL), axis=-1)
    new_peak = jnp.maximum(peak, block_peak)
    shifted = jnp.where(allowed, scores - new_peak[:, :, None], NEG_FILL)
    weights = jnp.exp(shifted)
    settled = jnp.where(allowed, shifted, 0.0)
    factor = jnp.exp(peak - new_peak)
    mass_new = mass * factor + jnp.sum(weights, axis=-1)
    moment_new = moment * factor + jnp.sum(weights * distance, axis=-1)
    spread_new = factor * (spread + (peak - new_peak) * mass) + jnp.sum(weights * settled, axis=-1)
    return (new_peak, mass_new, moment_new, spread_new)


def finish(state, col_count):
    disparity = state[2] / state[1] / col_count
    entropy = jnp.log(state[1]) - state[3] / state[1]
    return (disparity, entropy)


def local(left_image, right_image, conv_weight):
    row_count = left_image.shape[0] // 2
    col_count = left_image.shape[1] // 2
    border = jnp.stack([left_image[:, -1:, :], right_image[:, -1:, :]])
    border = from_behind(border, "col", 1)
    left_wide = jnp.concatenate([border[0], left_image], axis=1)
    right_wide = jnp.concatenate([border[1], right_image], axis=1)
    upper = from_behind(jnp.stack([left_wide[-1:], right_wide[-1:]]), "row", 1)
    left_full = jnp.concatenate([upper[0], left_wide], axis=0)
    right_full = jnp.concatenate([upper[1], right_wide], axis=0)
    left_feat = conv_taps(left_full, conv_weight, row_count, col_count)
    right_feat = conv_taps(right_full, conv_weight, row_count, col_count)
    position = lax.axis_index("col")
    start_state = empty_state(row_count, col_count)
    piece = lax.all_gather(right_feat, "col", axis=1, tiled=True)
    width_piece = piece.shape[1]
    anchor = position * col_count

    def visit(b, running):
        portion = lax.dynamic_slice_in_dim(piece, b * col_count, col_count, 1)
        return absorb(running, left_feat, portion, anchor - b * col_count)

    final = lax.fori_loop(0, width_piece // col_count, visit, start_state)
    return finish(final, col_count)


def solution(mesh):
    in_specs = (P("row", "col", None), P("row", "col", None), P())
    out_specs = (P("row", "col"), P("row", "col"))
    return jax.shard_map(local, mesh=mesh, in_specs=in_specs, out_specs=out_specs, check_vma=False)
```

profile of v0, /device:TPU:1, one launch (start us, length us, event | category | flops | bytes accessed | tf_op | source)
XLA Modules:
  0.0 227.8 jit_solution(3837790933711198921)
XLA Ops:
  8.8 4.9 %collective-permute-start = (bf16[2,8,1,128]{3,1,2,0:T(8,128)(2,1)S(1)}, bf16[2,8,1,128]{3,1,2,0:T(8,128)(2,1)S(1)}, u32[]{:S(2)}, u32[]{:S(2)}) collective-permute-start(bf16[2,8,1,128]{3,1,2,0:T(8,128)(2,1)S(1)} %pad_maximum_fusion.3), channel_id=1, source_target_pairs={{0,1},{1,2},{2,3},{3,4},{4,5},{5,6},{6,7},{7,8},{8,9},{9,10},{10,1... | collective-permute-start | bytes 12296 | tf_op jit(solution)/shard_map/ppermute | solution.py:12
  15.6 3.8 %collective-permute-start.1 = (bf16[2,1,513,128]{3,2,1,0:T(8,128)(2,1)S(1)}, bf16[2,1,513,128]{3,2,1,0:T(8,128)(2,1)}, u32[]{:S(2)}, u32[]{:S(2)}) collective-permute-start(bf16[2,1,513,128]{3,2,1,0:T(8,128)(2,1)S(1)} %pad_maximum_fusion.2), channel_id=1, source_target_pairs={{0,32},{32,64},{64,96},{96,128},{128,160},{160,192},{192,224},{1,3... | collective-permute-start | bytes 787976 | tf_op jit(solution)/shard_map/ppermute | solution.py:12
  19.4 2.6 %slice.131 = bf16[4,256,128]{2,1,0:T(8,128)(2,1)} slice(bf16[8,512,128]{2,1,0:T(8,128)(2,1)S(1)} %copy-done), slice={[0:7:2], [1:512:2], [0:128:1]} | slice | bytes 524288 | tf_op jit(solution)/shard_map/slice | solution.py:19
  22.0 2.6 %slice.129 = bf16[4,256,128]{2,1,0:T(8,128)(2,1)} slice(bf16[8,512,128]{2,1,0:T(8,128)(2,1)S(1)} %copy-done), slice={[0:7:2], [0:511:2], [0:128:1]} | slice | bytes 524288 | tf_op jit(solution)/shard_map/slice | solution.py:19
  24.6 2.7 %slice.137 = bf16[4,256,128]{2,1,0:T(8,128)(2,1)} slice(bf16[8,512,128]{2,1,0:T(8,128)(2,1)S(1)} %copy-done), slice={[1:8:2], [1:512:2], [0:128:1]} | slice | bytes 524288 | tf_op jit(solution)/shard_map/slice | solution.py:19
  27.4 2.7 %slice.135 = bf16[4,256,128]{2,1,0:T(8,128)(2,1)} slice(bf16[8,512,128]{2,1,0:T(8,128)(2,1)S(1)} %copy-done), slice={[1:8:2], [0:511:2], [0:128:1]} | slice | bytes 524288 | tf_op jit(solution)/shard_map/slice | solution.py:19
  30.4 2.7 %slice.133 = bf16[4,256,128]{2,1,0:T(8,128)(2,1)} slice(bf16[8,513,128]{2,1,0:T(8,128)(2,1)S(1)} %pad_maximum_fusion.1), slice={[1:8:2], [0:511:2], [0:128:1]} | slice | bytes 524288 | tf_op jit(solution)/shard_map/slice | solution.py:19
  33.1 2.6 %slice.127 = bf16[4,256,128]{2,1,0:T(8,128)(2,1)} slice(bf16[8,513,128]{2,1,0:T(8,128)(2,1)S(1)} %pad_maximum_fusion.1), slice={[0:7:2], [0:511:2], [0:128:1]} | slice | bytes 524288 | tf_op jit(solution)/shard_map/slice | solution.py:19
  37.0 2.6 %slice.125 = bf16[4,256,128]{2,1,0:T(8,128)(2,1)} slice(bf16[9,513,128]{2,1,0:T(8,128)(2,1)S(1)} %maximum_maximum_fusion), slice={[0:7:2], [2:513:2], [0:128:1]} | slice | bytes 524288 | tf_op jit(solution)/shard_map/slice | solution.py:19
  40.0 2.6 %slice.121 = bf16[4,256,128]{2,1,0:T(8,128)(2,1)} slice(bf16[9,513,128]{2,1,0:T(8,128)(2,1)S(1)} %maximum_maximum_fusion), slice={[0:7:2], [0:511:2], [0:128:1]} | slice | bytes 524288 | tf_op jit(solution)/shard_map/slice | solution.py:19
  51.7 2.6 %slice.145 = bf16[4,256,128]{2,1,0:T(8,128)(2,1)} slice(bf16[8,512,128]{2,1,0:T(8,128)(2,1)S(1)} %copy-done.1), slice={[0:7:2], [1:512:2], [0:128:1]} | slice | bytes 524288 | tf_op jit(solution)/shard_map/slice | solution.py:19
  54.3 2.6 %slice.144 = bf16[4,256,128]{2,1,0:T(8,128)(2,1)} slice(bf16[8,512,128]{2,1,0:T(8,128)(2,1)S(1)} %copy-done.1), slice={[0:7:2], [0:511:2], [0:128:1]} | slice | bytes 524288 | tf_op jit(solution)/shard_map/slice | solution.py:19
  58.3 2.7 %slice.146 = bf16[4,256,128]{2,1,0:T(8,128)(2,1)} slice(bf16[8,513,128]{2,1,0:T(8,128)(2,1)S(1)} %pad_maximum_fusion), slice={[1:8:2], [0:511:2], [0:128:1]} | slice | bytes 524288 | tf_op jit(solution)/shard_map/slice | solution.py:19
  61.0 2.6 %slice.143 = bf16[4,256,128]{2,1,0:T(8,128)(2,1)} slice(bf16[8,513,128]{2,1,0:T(8,128)(2,1)S(1)} %pad_maximum_fusion), slice={[0:7:2], [0:511:2], [0:128:1]} | slice | bytes 524288 | tf_op jit(solution)/shard_map/slice | solution.py:19
  70.4 85.2 %all-gather.2.cloned.1.call-done = bf16[4,8192,256]{2,1,0:T(8,128)(2,1)} async-done(((bf16[4,256,256]{2,1,0:T(8,128)(2,1)}), bf16[4,8192,256]{2,1,0:T(8,128)(2,1)}) %all-gather.2.cloned.1.call-update) | async-done | bytes 16777232 | tf_op jit(solution)/shard_map/all_gather | solution.py:77
  155.5 64.8 %while.20 = (s32[]{:T(128)}, f32[4,256]{1,0:T(4,128)S(1)}, f32[4,256]{1,0:T(4,128)S(1)}, f32[4,256]{1,0:T(4,128)S(1)}, f32[4,256]{1,0:T(4,128)S(1)}, /*index=5*/...) while((s32[]{:T(128)}, f32[4,256]{1,0:T(4,128)S(1)}, ...), condition=%wide.region_5.6_spmd.clone, body=%wide.region_0.5_spmd.clone.sunk | while | flops 137309440 | bytes 3955922 | solution.py:85
  157.7 1.4 select_reduce_fusion.2
  159.7 1.4 select_reduce_fusion.2
  163.8 1.4 select_reduce_fusion.2
  167.8 1.4 select_reduce_fusion.2
  171.9 1.4 select_reduce_fusion.2
  175.9 1.4 select_reduce_fusion.2
  180.0 1.4 select_reduce_fusion.2
  184.0 1.4 select_reduce_fusion.2
  188.1 1.4 select_reduce_fusion.2
  192.1 1.4 select_reduce_fusion.2
  196.2 1.4 select_reduce_fusion.2
  200.2 1.4 select_reduce_fusion.2
  204.3 1.4 select_reduce_fusion.2
  208.3 1.4 select_reduce_fusion.2
  212.4 1.4 select_reduce_fusion.2
  216.4 1.4 select_reduce_fusion.2
  (316 shorter events, 63.2 us)
Async XLA Ops:
  7.2 8.3 %copy-start.1 = (bf16[8,512,128]{2,1,0:T(8,128)(2,1)S(1)}, bf16[8,512,128]{2,1,0:T(8,128)(2,1)}, u32[]{:S(2)}) copy-start(bf16[8,512,128]{2,1,0:T(8,128)(2,1)} %param.5) | copy-start | bytes 3145732
  7.2 148.4 %all-gather.2.cloned.1.call-start = ((), (), s32[]{:S(2)}) async-start(), calls=%async_computation | async-start | bytes 17301504 | tf_op jit(solution)/shard_map/all_gather | solution.py:77
  8.8 5.7 %collective-permute-start = (bf16[2,8,1,128]{3,1,2,0:T(8,128)(2,1)S(1)}, bf16[2,8,1,128]{3,1,2,0:T(8,128)(2,1)S(1)}, u32[]{:S(2)}, u32[]{:S(2)}) collective-permute-start(bf16[2,8,1,128]{3,1,2,0:T(8,128)(2,1)S(1)} %pad_maximum_fusion.3), channel_id=1, source_target_pairs={{0,1},{1,2},{2,3},{3,4},{4,5},{5,6},{6,7},{7,8},{8,9},{9,10},{10,1... | collective-permute-start | bytes 12296 | tf_op jit(solution)/shard_map/ppermute | solution.py:12
  14.5 5.0 %copy-start = (bf16[8,512,128]{2,1,0:T(8,128)(2,1)S(1)}, bf16[8,512,128]{2,1,0:T(8,128)(2,1)}, u32[]{:S(2)}) copy-start(bf16[8,512,128]{2,1,0:T(8,128)(2,1)} %param.6) | copy-start | bytes 3145732
  15.6 20.1 %collective-permute-start.1 = (bf16[2,1,513,128]{3,2,1,0:T(8,128)(2,1)S(1)}, bf16[2,1,513,128]{3,2,1,0:T(8,128)(2,1)}, u32[]{:S(2)}, u32[]{:S(2)}) collective-permute-start(bf16[2,1,513,128]{3,2,1,0:T(8,128)(2,1)S(1)} %pad_maximum_fusion.2), channel_id=1, source_target_pairs={{0,32},{32,64},{64,96},{96,128},{128,160},{160,192},{192,224},{1,3... | collective-permute-start | bytes 787976 | tf_op jit(solution)/shard_map/ppermute | solution.py:12
  37.0 5.6 %copy-start.2 = (bf16[3,3,128,256]{3,2,1,0:T(8,128)(2,1)S(1)}, bf16[3,3,128,256]{3,2,1,0:T(8,128)(2,1)}, u32[]{:S(2)}) copy-start(bf16[3,3,128,256]{3,2,1,0:T(8,128)(2,1)} %param.7) | copy-start | bytes 1769476
  43.9 1.0 copy-start.12
  44.8 0.9 copy-start.10
  45.8 0.9 copy-start.8
  46.7 0.9 copy-start.5
  47.7 0.9 copy-start.6
  48.6 0.9 copy-start.3
  49.6 0.9 copy-start.13
  65.7 1.0 copy-start.11
  66.6 1.0 copy-start.7
  67.6 0.9 copy-start.4
  68.6 0.9 copy-start.9
Sparse Core Ops, SparseCore 0:
  51.8 103.7 all-gather.1
where the time goes:
time: 230 us; the launch traced here: 228 us
  waiting for transfers between devices  85.9 us (37%)
  matrix products  51.6 us (22%)
  local copies, waits for them, and re-layouts  44.5 us (19%)
  other arithmetic  20.5 us (9%)
  between operations  14.3 us (6%)
  starting transfers between devices  8.8 us (4%)
    all_gather x1, waiting for transfers between devices, local(): piece = lax.all_gather(right_feat, 'col', axis=1, tiled=True)  85.2 us
    dot_general x32, matrix products, absorb(): jnp.einsum('rif,rjf->rij', query, panel_keys, preferred_element_type=jnp....  44.9 us
    slice x18, local copies, waits for them, and re-layouts, conv_taps(): window = padded[a:a + 2 * row_count - 1:2, b:b + 2 * col_count - 1:2, :]  34.4 us
    reduce_sum x32, other arithmetic, absorb(): jnp.sum(weights * settled, axis=-1)  12.7 us
    ppermute x2, starting transfers between devices, from_behind(): return lax.ppermute(array, axis, pairs)  8.76 us
    unnamed x28, local copies, waits for them, and re-layouts  7.4 us
    dot_general x18, matrix products, conv_taps(): jnp.dot(window.reshape(row_count * col_count, -1), weights[a, b], preferr...  6.72 us
  transfers between devices with their start and end apart: 3, of which 2 were waited for; matrix products, arithmetic and copies ran while one was open for 14% of the time, Pallas kernels for 0%

commit v1 on v0

--- a/solution.py
+++ b/solution.py
@@ -74,7 +74,16 @@
     right_feat = conv_taps(right_full, conv_weight, row_count, col_count)
     position = lax.axis_index("col")
     start_state = empty_state(row_count, col_count)
-    piece = lax.all_gather(right_feat, "col", axis=1, tiled=True)
+
+    def treat_inputs(block_here):
+        cards = []
+        for _ in range(lax.axis_size("col")):
+            cards.append(block_here)
+        return jnp.concatenate(
+            lax.all_to_all(jnp.stack(cards), "col", split_axis=0, concat_axis=0), axis=1
+        )
+
+    piece = treat_inputs(right_feat)
     width_piece = piece.shape[1]
     anchor = position * col_count
 

time: 230 us -> 502 us (2.18)
  the two profiles are of different devices: /device:TPU:1 before, /device:TPU:102 now
where the time goes in v1:
time: 502 us; the launch traced here: 500 us
  waiting for transfers between devices  358 us (71%)
  local copies, waits for them, and re-layouts  52.2 us (10%)
  matrix products  49.9 us (10%)
  other arithmetic  20.4 us (4%)
  starting transfers between devices  16.3 us (3%)
    all_to_all x1, waiting for transfers between devices, treat_inputs(): lax.all_to_all(jnp.stack(cards), 'col', split_axis=0, concat_axis=0)  355 us
    dot_general x32, matrix products, absorb(): jnp.einsum('rif,rjf->rij', query, panel_keys, preferred_element_type=jnp....  44.9 us
    slice x18, local copies, waits for them, and re-layouts, conv_taps(): window = padded[a:a + 2 * row_count - 1:2, b:b + 2 * col_count - 1:2, :]  25.4 us
    all_to_all x1, local copies, waits for them, and re-layouts, treat_inputs(): lax.all_to_all(jnp.stack(cards), 'col', split_axis=0, concat_axis=0)  13.9 us
    reduce_sum x32, other arithmetic, absorb(): jnp.sum(weights * settled, axis=-1)  12.6 us
  transfers between devices with their start and end apart: 3, of which 2 were waited for; matrix products, arithmetic and copies ran while one was open for 6% of the time, Pallas kernels for 0%

profile of v1, /device:TPU:102, one launch (start us, length us, event | category | flops | bytes accessed | tf_op | source)
XLA Modules:
  0.0 499.7 jit_solution(16991476140624722128)
XLA Ops:
  2.2 1.9 collective-permute-start
  4.1 3.0 collective-permute-done
  8.2 5.0 %collective-permute-start.1 = (bf16[2,1,513,128]{3,2,1,0:T(8,128)(2,1)S(1)}, bf16[2,1,513,128]{3,2,1,0:T(8,128)(2,1)S(1)}, u32[]{:S(2)}, u32[]{:S(2)}) collective-permute-start(bf16[2,1,513,128]{3,2,1,0:T(8,128)(2,1)S(1)} %pad_maximum_fusion.2), channel_id=1, source_target_pairs={{0,32},{32,64},{64,96},{96,128},{128,160},{160,192},{192,224},{1,3... | collective-permute-start | bytes 787976 | tf_op jit(solution)/shard_map/ppermute | solution.py:12
  13.2 2.6 slice.129
  16.8 2.7 slice.137
  19.8 2.6 slice.127
  22.4 2.7 slice.133
  31.8 5.9 %stack.27 = bf16[32,4,256,256]{3,2,1,0:T(8,128)(2,1)} broadcast(bf16[4,256,256]{2,1,0:T(8,128)(2,1)S(1)} %bitcast.108), dimensions={1,2,3} | broadcast | bytes 17301504 | tf_op jit(solution)/shard_map/stack | solution.py:83
  37.8 9.3 %all-to-all-start = ((bf16[32,4,256,256]{3,2,1,0:T(8,128)(2,1)}), bf16[32,4,256,256]{3,2,1,0:T(8,128)(2,1)}, u32[]{:S(2)}, u32[]{:S(2)}) async-start(bf16[32,4,256,256]{3,2,1,0:T(8,128)(2,1)} %stack.27), calls=%async_computation | async-start | bytes 33554432 | tf_op jit(solution)/shard_map/all_to_all | solution.py:83
  47.1 2.6 slice.144
  50.7 2.7 slice.148
  53.7 2.6 slice.143
  56.3 2.7 slice.146
  65.7 354.6 %all-to-all-done = bf16[32,4,256,256]{3,2,1,0:T(8,128)(2,1)} async-done(((bf16[32,4,256,256]{3,2,1,0:T(8,128)(2,1)}), bf16[32,4,256,256]{3,2,1,0:T(8,128)(2,1)}, u32[]{:S(2)}, u32[]{:S(2)}) %all-to-all-start) | async-done | bytes 16777248 | tf_op jit(solution)/shard_map/all_to_all | solution.py:83
  420.3 13.9 %copy.20 = bf16[32,4,256,256]{3,2,0,1:T(8,128)(2,1)} copy(bf16[32,4,256,256]{3,2,1,0:T(8,128)(2,1)} %all-to-all-done) | data formatting | bytes 33554432 | tf_op jit(solution)/shard_map/all_to_all | solution.py:83
  434.2 64.9 %while.20 = (s32[]{:T(128)}, f32[4,256]{1,0:T(4,128)S(1)}, f32[4,256]{1,0:T(4,128)S(1)}, f32[4,256]{1,0:T(4,128)S(1)}, f32[4,256]{1,0:T(4,128)S(1)}, /*index=5*/...) while((s32[]{:T(128)}, f32[4,256]{1,0:T(4,128)S(1)}, ...), condition=%wide.region_5.6_spmd.clone, body=%wide.region_0.5_spmd.clone.sunk | while | flops 137309440 | bytes 3955914 | solution.py:94
  434.3 1.4 select_reduce_fusion.2
  440.4 1.4 select_reduce_fusion.2
  442.4 1.4 select_reduce_fusion.2
  444.4 1.4 select_reduce_fusion.2
  446.4 1.4 select_reduce_fusion.2
  448.5 1.4 select_reduce_fusion.2
  454.6 1.4 select_reduce_fusion.2
  456.6 1.4 select_reduce_fusion.2
  458.6 1.4 select_reduce_fusion.2
  460.6 1.4 select_reduce_fusion.2
  462.7 1.4 select_reduce_fusion.2
  468.8 1.4 select_reduce_fusion.2
  470.8 1.4 select_reduce_fusion.2
  474.8 1.4 select_reduce_fusion.2
  485.0 1.4 select_reduce_fusion.2
  489.0 1.4 select_reduce_fusion.2
  (311 shorter events, 59.0 us)
Async XLA Ops:
  0.6 7.5 %copy-start = (bf16[8,512,128]{2,1,0:T(8,128)(2,1)S(1)}, bf16[8,512,128]{2,1,0:T(8,128)(2,1)}, u32[]{:S(2)}) copy-start(bf16[8,512,128]{2,1,0:T(8,128)(2,1)} %param.6) | copy-start | bytes 3145732
  2.2 4.9 collective-permute-start
  8.2 16.9 %collective-permute-start.1 = (bf16[2,1,513,128]{3,2,1,0:T(8,128)(2,1)S(1)}, bf16[2,1,513,128]{3,2,1,0:T(8,128)(2,1)S(1)}, u32[]{:S(2)}, u32[]{:S(2)}) collective-permute-start(bf16[2,1,513,128]{3,2,1,0:T(8,128)(2,1)S(1)} %pad_maximum_fusion.2), channel_id=1, source_target_pairs={{0,32},{32,64},{64,96},{96,128},{128,160},{160,192},{192,224},{1,3... | collective-permute-start | bytes 787976 | tf_op jit(solution)/shard_map/ppermute | solution.py:12
  25.4 1.2 copy-start.2
  27.2 1.0 copy-start.7
  28.1 0.9 copy-start.4
  29.3 1.0 copy-start.5
  30.6 1.0 copy-start.10
  37.8 9.4 %copy-start.1 = (bf16[8,512,128]{2,1,0:T(8,128)(2,1)S(1)}, bf16[8,512,128]{2,1,0:T(8,128)(2,1)}, u32[]{:S(2)}) copy-start(bf16[8,512,128]{2,1,0:T(8,128)(2,1)} %param.5) | copy-start | bytes 3145732
  37.8 382.5 %all-to-all-start = ((bf16[32,4,256,256]{3,2,1,0:T(8,128)(2,1)}), bf16[32,4,256,256]{3,2,1,0:T(8,128)(2,1)}, u32[]{:S(2)}, u32[]{:S(2)}) async-start(bf16[32,4,256,256]{3,2,1,0:T(8,128)(2,1)} %stack.27), calls=%async_computation | async-start | bytes 33554432 | tf_op jit(solution)/shard_map/all_to_all | solution.py:83
  61.0 1.0 copy-start.8
  62.0 0.9 copy-start.3
  63.2 1.0 copy-start.6
  64.4 1.0 copy-start.9
